TPU v7x, 32 devices: a whole 2x2x4 slice. The times are simulated.
32 devices in a mesh: row: 4 (over z), col: 4 (over y, core), pix: 2 (over x).
Axes of the slice: x: 2, y: 2, z: 4, core: 2. Of those that a mesh axis runs over, the one named last changes fastest.
Arguments:
- sample_frames: bfloat16 [4096, 16384], P(('row', 'col'), 'pix'), may hold values from 0.14 to 26
- reference_frames: bfloat16 [4096, 16384], P(('row', 'col'), 'pix'), may hold values from 0.14 to 26
- gain: float32 [16384], P('pix'), may hold values from 0.5 to 2
- flat: float32 [16384], P('pix'), may hold values from 0.6 to 1.6
- qbin: int32 [16384], P('pix'), may hold values from 0 to 31
- region: int32 [16384], P('pix'), may hold values 0 or 1
- live: int32 [16384], P('pix'), may hold values 0 or 1
Outputs:
- twotime: float32 [4096, 4, 4, 256], P('row', None, 'col', 'pix')
All inputs are finite; a program needn't handle non-finite values. No bound on the sum of `region` or of `live` on one device may be relied on, other than what follows from the above.
Results may differ from a plain program's by a relative error of at most 0.0039.
Values may be sent and summed in bfloat16 or wider, within the bound.
No kernel may reach another device: no remote copies, remote signals or barrier semaphores. Data moves between devices by JAX's collectives and lax.ppermute only.
A program may use at most 128 MiB of HBM per device.

v0:
```python
import math
import jax
import jax.numpy as jnp
from jax import lax
from jax.sharding import PartitionSpec as P

QBINS = 32


def on_device(sample_frames, reference_frames, gain, flat, qbin, region, live):
    block = sample_frames.shape[0]
    factor = gain / flat
    select = (qbin[None, :] == jnp.arange(QBINS, dtype=jnp.int32)[:, None]).astype(jnp.float32)
    ref_select = select * (live * (1 - region)).astype(jnp.float32)[None, :]
    sample_weight = (live * region).astype(jnp.float32)
    corrected_sample = sample_frames.astype(jnp.float32) * factor
    corrected_reference = reference_frames.astype(jnp.float32) * factor
    sums_sample = jnp.dot(corrected_sample, ref_select.T, precision=lax.Precision.HIGHEST)
    sums_reference = jnp.dot(corrected_reference, ref_select.T, precision=lax.Precision.HIGHEST)
    counts = jnp.sum(ref_select, axis=1)
    sums_sample, sums_reference, counts = lax.psum((sums_sample, sums_reference, counts), "pix")
    mean_sample = (sums_sample + 1.0) / (counts + 1.0)
    mean_reference = (sums_reference + 1.0) / (counts + 1.0)
    spread_sample = jnp.dot(mean_sample, select, precision=lax.Precision.HIGHEST)
    spread_reference = jnp.dot(mean_reference, select, precision=lax.Precision.HIGHEST)
    delta_sample = ((corrected_sample / spread_sample - 1.0) * sample_weight).astype(jnp.bfloat16)
    delta_reference = (corrected_reference / spread_reference - 1.0).astype(jnp.bfloat16)
    sample_rows = lax.all_gather(delta_sample, "col", axis=0, tiled=True)
    partial_value = lax.dot_general(
        sample_rows,
        lax.all_gather(delta_reference, "row", axis=0, tiled=True),
        (((1,), (1,)), ((), ())),
        preferred_element_type=jnp.float32,
    )
    groups = lax.axis_size("row")
    scale = 1.0 / math.sqrt(gain.shape[0] * lax.axis_size("pix"))
    partial_value = (partial_value * scale).reshape(sample_rows.shape[0], groups, block)
    whole = lax.psum(partial_value, "pix")
    width = block // lax.axis_size("pix")
    mine = lax.dynamic_slice_in_dim(whole, lax.axis_index("pix") * width, width, 2)
    return mine[:, :, None, :]


def solution(mesh):
    return jax.shard_map(
        on_device,
        mesh=mesh,
        in_specs=(
            P(("row", "col"), "pix"),
            P(("row", "col"), "pix"),
            P("pix"),
            P("pix"),
            P("pix"),
            P("pix"),
            P("pix"),
        ),
        out_specs=P("row", None, "col", "pix"),
        check_vma=False,
    )
```

profile of v0, /device:TPU:0, one launch (start us, length us, event | category | flops | bytes accessed | tf_op | source)
XLA Modules:
  0.0 598.4 jit_solution(18286605986021742596)
XLA Ops:
  6.5 0.0 copy-start
  6.5 0.0 all-reduce.6.cloned.1.call-start
  6.5 0.8 multiply_convert_fusion.1
  7.3 0.8 div.23
  8.1 1.5 select_reduce_fusion
  9.6 9.2 %fusion.5 = f32[256,32]{1,0:T(8,128)} fusion(bf16[256,8192]{1,0:T(8,128)(2,1)} %param.8, f32[8192]{0:T(1024)S(1)} %div.23, f32[8192]{0:T(1024)S(1)} %get-tuple-element.8, s32[8192]{0:T(1024)} %param.11), kind=kOutput, calls=%fused_computation.8 | convolution fusion | flops 810024960 | bytes 4325376 | tf_op jit(solution)/shard_map/dot_general | solution.py:19
  18.8 9.2 %fusion.6 = f32[256,32]{1,0:T(8,128)} fusion(bf16[256,8192]{1,0:T(8,128)(2,1)} %param.7, f32[8192]{0:T(1024)S(1)} %div.23, f32[8192]{0:T(1024)S(1)} %get-tuple-element.8, s32[8192]{0:T(1024)} %param.11), kind=kOutput, calls=%fused_computation.10 | convolution fusion | flops 810024960 | bytes 4325376 | tf_op jit(solution)/shard_map/dot_general | solution.py:18
  28.0 0.0 all-reduce.6.cloned.1.call-update
  28.1 0.0 all-gather.3.cloned.1.call-start
  28.1 26.4 %all-reduce.6.cloned.1.call-done = (f32[256,32]{1,0:T(8,128)}, f32[32]{0:T(128)}, f32[256,32]{1,0:T(8,128)}) async-done(((f32[256,32]{1,0:T(8,128)}, f32[32]{0:T(128)}, f32[256,32]{1,0:T(8,128)}), (f32[256,32]{1,0:T(8,128)}, f32[32]{0:T(128)}, f32[256,32]{1,0:T(8,128)})) %all-reduce.6.cloned.1.call-update) | async-done | bytes 65680 | tf_op jit(solution)/shard_map/psum | solution.py:21
  54.5 0.6 broadcast_add_fusion
  55.1 0.0 copy-done
  55.1 0.0 copy-start.1
  55.1 7.9 %fusion.4 = bf16[256,8192]{1,0:T(8,128)(2,1)} fusion(bf16[256,8192]{1,0:T(8,128)(2,1)} %param.7, f32[8192]{0:T(1024)S(1)} %get-tuple-element.9, f32[8192]{0:T(1024)S(1)} %div.23, s32[8192]{0:T(1024)S(1)} %copy-done, f32[256,32]{1,0:T(8,128)} %get-tuple-element.5, f32[32]{0:T(128)S(1)} %broadcast_add_fusion), kind=kOutput, calls=%fused_computation.6 | convolution fusion | flops 818167808 | bytes 8519808 | tf_op jit(solution)/shard_map/dot_general | solution.py:24
  63.0 0.0 all-gather.3.cloned.1.call-update
  63.0 0.2 all-gather.5.cloned.1.call-start
  63.3 0.0 copy-done.1
  63.3 7.6 %fusion.1 = bf16[256,8192]{1,0:T(8,128)(2,1)} fusion(bf16[256,8192]{1,0:T(8,128)(2,1)} %param.8, f32[8192]{0:T(1024)S(1)} %div.23, s32[8192]{0:T(1024)S(1)} %copy-done, f32[256,32]{1,0:T(8,128)S(1)} %copy-done.1, f32[32]{0:T(128)S(1)} %broadcast_add_fusion), kind=kOutput, calls=%fused_computation.2 | convolution fusion | flops 816070656 | bytes 8487040 | tf_op jit(solution)/shard_map/dot_general | solution.py:25
  70.9 0.0 all-gather.5.cloned.1.call-update
  70.9 0.0 all-reduce.4.cloned.1.call-start
  70.9 98.4 %all-gather.3.cloned.1.call-done = bf16[1024,8192]{1,0:T(8,128)(2,1)} async-done(((bf16[256,8192]{1,0:T(8,128)(2,1)}), bf16[1024,8192]{1,0:T(8,128)(2,1)}) %all-gather.3.cloned.1.call-update) | async-done | bytes 16777232 | tf_op jit(solution)/shard_map/all_gather | solution.py:28
  169.3 288.5 %all-gather.5.cloned.1.call-done = bf16[1024,8192]{1,0:T(8,128)(2,1)} async-done(((bf16[256,8192]{1,0:T(8,128)(2,1)}), bf16[1024,8192]{1,0:T(8,128)(2,1)}) %all-gather.5.cloned.1.call-update) | async-done | bytes 16777232 | tf_op jit(solution)/shard_map/all_gather | solution.py:31
  457.8 24.3 %convolution_multiply_fusion = f32[1024,1024]{0,1:T(8,128)} fusion(bf16[1024,8192]{1,0:T(8,128)(2,1)} %all-gather.3.cloned.1.call-done, bf16[1024,8192]{1,0:T(8,128)(2,1)} %all-gather.5.cloned.1.call-done), kind=kOutput, calls=%fused_computation.13 | convolution fusion | flops 17180917760 | bytes 37748736 | tf_op jit(solution)/shard_map/dot_general | solution.py:29
  482.1 0.0 all-reduce.4.cloned.1.call-update
  482.1 106.2 %all-reduce.4.cloned.1.call-done = f32[1024,4,256]{0,2,1:T(8,128)} async-done(((f32[1024,4,256]{0,2,1:T(8,128)}), f32[1024,4,256]{0,2,1:T(8,128)}) %all-reduce.4.cloned.1.call-update) | async-done | bytes 4194320 | tf_op jit(solution)/shard_map/psum | solution.py:38
  588.3 1.7 constant_dynamic-slice_fusion
  590.1 1.8 copy.9
Async XLA Ops:
  6.5 48.6 %copy-start = (s32[8192]{0:T(1024)S(1)}, s32[8192]{0:T(1024)}, u32[]{:S(2)}) copy-start(s32[8192]{0:T(1024)} %param.11) | copy-start | bytes 98308
  6.5 48.0 %all-reduce.6.cloned.1.call-start = ((), (), s32[]{:S(2)}) async-start(), calls=%async_computation.3 | async-start | bytes 525312 | tf_op jit(solution)/shard_map/psum | solution.py:21
  28.1 141.3 %all-gather.3.cloned.1.call-start = ((), (), s32[]{:S(2)}) async-start(), calls=%async_computation | async-start | bytes 20971520 | tf_op jit(solution)/shard_map/all_gather | solution.py:28
  55.1 8.2 %copy-start.1 = (f32[256,32]{1,0:T(8,128)S(1)}, f32[256,32]{1,0:T(8,128)}, u32[]{:S(2)}) copy-start(f32[256,32]{1,0:T(8,128)} %get-tuple-element.7) | copy-start | bytes 98308
  63.0 394.8 %all-gather.5.cloned.1.call-start = ((), (), s32[]{:S(2)}) async-start(), calls=%async_computation.1 | async-start | bytes 20971520 | tf_op jit(solution)/shard_map/all_gather | solution.py:31
  70.9 517.4 %all-reduce.4.cloned.1.call-start = ((), (), s32[]{:S(2)}) async-start(), calls=%async_computation.2 | async-start | bytes 8388608 | tf_op jit(solution)/shard_map/psum | solution.py:38
Sparse Core Ops, SparseCore 0:
  28.2 26.2 all-reduce.5
  63.2 106.1 all-gather.2
  171.0 286.7 all-gather.4
  482.3 106.0 all-reduce.3
where the time goes:
time: 599 us; the launch traced here: 598 us
  waiting for transfers between devices  519 us (87%)
  matrix products  58.3 us (10%)
  between operations  13.2 us (2%)
    all_gather x1, waiting for transfers between devices, on_device(): lax.all_gather(delta_reference, 'row', axis=0, tiled=True)  288 us
    psum x1, waiting for transfers between devices, on_device(): whole = lax.psum(partial_value, 'pix')  106 us
    all_gather x1, waiting for transfers between devices, on_device(): sample_rows = lax.all_gather(delta_sample, 'col', axis=0, tiled=True)  98.4 us
    psum x1, waiting for transfers between devices, on_device(): lax.psum((sums_sample, sums_reference, counts), 'pix')  26.4 us
    dot_general x1, matrix products, on_device(): lax.dot_general(sample_rows, lax.all_gather(delta_reference, 'row', axis=...  24.3 us
  transfers between devices with their start and end apart: 4, of which 4 were waited for; matrix products, arithmetic and copies ran while one was open for 1% of the time, Pallas kernels for 0%

commit v1 on v0

--- a/solution.py
+++ b/solution.py
@@ -25,7 +25,12 @@
     spread_reference = jnp.dot(mean_reference, select, precision=lax.Precision.HIGHEST)
     delta_sample = ((corrected_sample / spread_sample - 1.0) * sample_weight).astype(jnp.bfloat16)
     delta_reference = (corrected_reference / spread_reference - 1.0).astype(jnp.bfloat16)
-    sample_rows = lax.all_gather(delta_sample, "col", axis=0, tiled=True)
+    ring = [delta_sample]
+    for hop in range(3):
+        ring.append(lax.ppermute(ring[-1], "col", [(dev, (dev + 1) % 4) for dev in range(4)]))
+    sample_rows = jnp.roll(
+        jnp.concatenate(ring[::-1], axis=0), (lax.axis_index("col") + 1) * ring[0].shape[0], axis=0
+    )
     partial_value = lax.dot_general(
         sample_rows,
         lax.all_gather(delta_reference, "row", axis=0, tiled=True),

time: 599 us -> 491 us (0.82)
  waiting for transfers between devices: 519 us -> 381 us
  local copies, waits for them, and re-layouts: 3.55 us -> 35.1 us
    all_gather x1, waiting for transfers between devices: 288 us -> 105 us  [on_device(): lax.all_gather(delta_reference, 'row', axis=0, tiled=True)]
    ppermute x0 -> x3, waiting for transfers between devices: none -> 144 us  [on_device(): lax.ppermute(ring[-1], 'col', [(dev, (dev + 1) % 4) for dev in range(4)])]
    all_gather x1 -> x0, waiting for transfers between devices: 98.4 us -> none  [on_device(): sample_rows = lax.all_gather(delta_sample, 'col', axis=0, tiled=True)]
    unnamed x4 -> x19, local copies, waits for them, and re-layouts: 0.01 us -> 29.3 us
  transfers between devices with their start and end apart: 4 -> 6, of which waited for: 4 -> 6; matrix products, arithmetic and copies ran while one was open for 1% -> 7% of each run, Pallas kernels for 0% -> 0%
where the time goes in v1:
time: 491 us
  waiting for transfers between devices  381 us (78%)
  matrix products  57 us (12%)
  local copies, waits for them, and re-layouts  35.1 us (7%)
  between operations  13.2 us (3%)
    ppermute x3, waiting for transfers between devices, on_device(): lax.ppermute(ring[-1], 'col', [(dev, (dev + 1) % 4) for dev in range(4)])  144 us
    psum x1, waiting for transfers between devices, on_device(): whole = lax.psum(partial_value, 'pix')  106 us
    all_gather x1, waiting for transfers between devices, on_device(): lax.all_gather(delta_reference, 'row', axis=0, tiled=True)  105 us
    unnamed x19, local copies, waits for them, and re-layouts  29.3 us
    psum x1, waiting for transfers between devices, on_device(): lax.psum((sums_sample, sums_reference, counts), 'pix')  26.4 us
    dot_general x1, matrix products, on_device(): lax.dot_general(sample_rows, lax.all_gather(delta_reference, 'row', axis=...  24.3 us
  transfers between devices with their start and end apart: 6, of which 6 were waited for; matrix products, arithmetic and copies ran while one was open for 7% of the time, Pallas kernels for 0%

profile of v1, /device:TPU:0, one launch (start us, length us, event | category | flops | bytes accessed | tf_op | source)
XLA Modules:
  0.0 490.8 jit_solution(15064264575936679225)
XLA Ops:
  6.5 0.8 multiply_convert_fusion
  7.3 0.8 div.23
  8.1 1.6 select_reduce_fusion
  9.7 9.2 %fusion.7 = f32[256,32]{1,0:T(8,128)} fusion(bf16[256,8192]{1,0:T(8,128)(2,1)} %param.8, f32[8192]{0:T(1024)S(1)} %div.23, f32[8192]{0:T(1024)S(1)} %get-tuple-element.9, s32[8192]{0:T(1024)} %param.11), kind=kOutput, calls=%fused_computation.10 | convolution fusion | flops 810024960 | bytes 4325376 | tf_op jit(solution)/shard_map/dot_general | solution.py:19
  18.9 9.2 %fusion.8 = f32[256,32]{1,0:T(8,128)} fusion(bf16[256,8192]{1,0:T(8,128)(2,1)} %param.7, f32[8192]{0:T(1024)S(1)} %div.23, f32[8192]{0:T(1024)S(1)} %get-tuple-element.9, s32[8192]{0:T(1024)} %param.11), kind=kOutput, calls=%fused_computation.12 | convolution fusion | flops 810024960 | bytes 4325376 | tf_op jit(solution)/shard_map/dot_general | solution.py:18
  28.1 0.0 all-reduce.6.cloned.1.call-update
  28.2 0.0 all-gather.2.cloned.1.call-start
  28.2 26.4 %all-reduce.6.cloned.1.call-done = (f32[256,32]{1,0:T(8,128)}, f32[32]{0:T(128)}, f32[256,32]{1,0:T(8,128)}) async-done(((f32[256,32]{1,0:T(8,128)}, f32[32]{0:T(128)}, f32[256,32]{1,0:T(8,128)}), (f32[256,32]{1,0:T(8,128)}, f32[32]{0:T(128)}, f32[256,32]{1,0:T(8,128)})) %all-reduce.6.cloned.1.call-update) | async-done | bytes 65680 | tf_op jit(solution)/shard_map/psum | solution.py:21
  54.6 0.7 broadcast_add_fusion
  55.3 7.7 %fusion.3 = bf16[256,8192]{1,0:T(8,128)(2,1)} fusion(bf16[256,8192]{1,0:T(8,128)(2,1)} %param.8, f32[8192]{0:T(1024)S(1)} %div.23, s32[8192]{0:T(1024)S(1)} %copy-done.4, f32[256,32]{1,0:T(8,128)} %get-tuple-element.5, f32[32]{0:T(128)S(1)} %broadcast_add_fusion), kind=kOutput, calls=%fused_computation.4 | convolution fusion | flops 816070656 | bytes 8487040 | tf_op jit(solution)/shard_map/dot_general | solution.py:25
  63.0 0.0 all-gather.2.cloned.1.call-update
  63.0 0.2 all-reduce.4.cloned.1.call-start
  63.3 6.6 %fusion.6 = bf16[256,8192]{1,0:T(8,128)(2,1)S(1)} fusion(bf16[256,8192]{1,0:T(8,128)(2,1)} %param.7, f32[8192]{0:T(1024)S(1)} %get-tuple-element.8, f32[8192]{0:T(1024)S(1)} %div.23, s32[8192]{0:T(1024)S(1)} %copy-done.4, f32[256,32]{1,0:T(8,128)S(1)} %copy-done.5, f32[32]{0:T(128)S(1)} %broadcast_add_fusion), kind=kOutput, calls=%fused_computation.8 | convolution fusion | flops 818167808 | bytes 8519808 | tf_op jit(solution)/shard_map/dot_general | solution.py:24
  69.8 2.1 copy-done
  72.0 47.9 %collective-permute-done = bf16[256,8192]{1,0:T(8,128)(2,1)S(1)} collective-permute-done((bf16[256,8192]{1,0:T(8,128)(2,1)S(1)}, bf16[256,8192]{1,0:T(8,128)(2,1)S(1)}, u32[]{:S(2)}, u32[]{:S(2)}) %collective-permute-start) | collective-permute-done | bytes 4194336 | tf_op jit(solution)/shard_map/ppermute | solution.py:30
  119.9 2.0 copy-done.2
  121.9 48.0 %collective-permute-done.1 = bf16[256,8192]{1,0:T(8,128)(2,1)} collective-permute-done((bf16[256,8192]{1,0:T(8,128)(2,1)S(1)}, bf16[256,8192]{1,0:T(8,128)(2,1)}, u32[]{:S(2)}, u32[]{:S(2)}) %collective-permute-start.1) | collective-permute-done | bytes 4194336 | tf_op jit(solution)/shard_map/ppermute | solution.py:30
  169.9 48.2 %collective-permute-done.2 = bf16[256,8192]{1,0:T(8,128)(2,1)} collective-permute-done((bf16[256,8192]{1,0:T(8,128)(2,1)}, bf16[256,8192]{1,0:T(8,128)(2,1)}, u32[]{:S(2)}, u32[]{:S(2)}) %collective-permute-start.2) | collective-permute-done | bytes 4194336 | tf_op jit(solution)/shard_map/ppermute | solution.py:30
  218.2 4.6 constant_dynamic-update-slice_fusion.7
  222.8 4.7 constant_dynamic-update-slice_fusion.6
  227.5 2.2 constant_dynamic-update-slice_fusion.5
  229.8 2.2 constant_dynamic-update-slice_fusion.4
  232.0 4.6 constant_dynamic-update-slice_fusion.3
  236.5 4.6 constant_dynamic-update-slice_fusion.2
  241.1 2.2 constant_dynamic-update-slice_fusion.1
  243.4 2.2 constant_dynamic-update-slice_fusion
  245.6 104.6 %all-gather.2.cloned.1.call-done = bf16[1024,8192]{1,0:T(8,128)(2,1)} async-done(((bf16[256,8192]{1,0:T(8,128)(2,1)}), bf16[1024,8192]{1,0:T(8,128)(2,1)}) %all-gather.2.cloned.1.call-update) | async-done | bytes 16777232 | tf_op jit(solution)/shard_map/all_gather | solution.py:36
  350.2 24.3 %fusion.11 = f32[1024,1024]{0,1:T(8,128)} fusion(bf16[1024,8192]{1,0:T(8,128)(2,1)} %all-gather.2.cloned.1.call-done, bf16[2048,8192]{1,0:T(8,128)(2,1)} %constant_dynamic-update-slice_fusion, s32[]{:T(128)S(6)} %select_n.17), kind=kOutput, calls=%fused_computation.15 | convolution fusion | flops 17180917760 | bytes 37748740 | tf_op jit(solution)/shard_map/dot_general | solution.py:34
  374.5 0.0 all-reduce.4.cloned.1.call-update
  374.5 106.2 %all-reduce.4.cloned.1.call-done = f32[1024,4,256]{0,2,1:T(8,128)} async-done(((f32[1024,4,256]{0,2,1:T(8,128)}), f32[1024,4,256]{0,2,1:T(8,128)}) %all-reduce.4.cloned.1.call-update) | async-done | bytes 4194320 | tf_op jit(solution)/shard_map/psum | solution.py:43
  480.7 1.7 constant_dynamic-slice_fusion
  482.4 1.8 copy.9
  (14 shorter events, 0.0 us)
Async XLA Ops:
  6.5 48.7 %copy-start.4 = (s32[8192]{0:T(1024)S(1)}, s32[8192]{0:T(1024)}, u32[]{:S(2)}) copy-start(s32[8192]{0:T(1024)} %param.11) | copy-start | bytes 98308
  6.5 48.1 %all-reduce.6.cloned.1.call-start = ((), (), s32[]{:S(2)}) async-start(), calls=%async_computation.2 | async-start | bytes 525312 | tf_op jit(solution)/shard_map/psum | solution.py:21
  28.2 322.0 %all-gather.2.cloned.1.call-start = ((), (), s32[]{:S(2)}) async-start(), calls=%async_computation | async-start | bytes 20971520 | tf_op jit(solution)/shard_map/all_gather | solution.py:36
  55.3 8.0 %copy-start.5 = (f32[256,32]{1,0:T(8,128)S(1)}, f32[256,32]{1,0:T(8,128)}, u32[]{:S(2)}) copy-start(f32[256,32]{1,0:T(8,128)} %get-tuple-element.7) | copy-start | bytes 98308
  63.0 417.7 %all-reduce.4.cloned.1.call-start = ((), (), s32[]{:S(2)}) async-start(), calls=%async_computation.1 | async-start | bytes 8388608 | tf_op jit(solution)/shard_map/psum | solution.py:43
  69.8 2.1 copy-start
  72.0 47.9 %collective-permute-start = (bf16[256,8192]{1,0:T(8,128)(2,1)S(1)}, bf16[256,8192]{1,0:T(8,128)(2,1)S(1)}, u32[]{:S(2)}, u32[]{:S(2)}) collective-permute-start(bf16[256,8192]{1,0:T(8,128)(2,1)S(1)} %fusion.6), channel_id=1, source_target_pairs={{0,2},{2,4},{4,6},{6,0},{1,3},{3,5},{5,7},{7,1},{8,10},{10,12},{12... | collective-permute-start | bytes 12582920 | tf_op jit(solution)/shard_map/ppermute | solution.py:30
  119.9 2.0 copy-start.2
  121.9 48.0 %collective-permute-start.1 = (bf16[256,8192]{1,0:T(8,128)(2,1)S(1)}, bf16[256,8192]{1,0:T(8,128)(2,1)}, u32[]{:S(2)}, u32[]{:S(2)}) collective-permute-start(bf16[256,8192]{1,0:T(8,128)(2,1)S(1)} %collective-permute-done), channel_id=1, source_target_pairs={{0,2},{2,4},{4,6},{6,0},{1,3},{3,5},{5,7},{7,1},{8,10},{10,12},{12... | collective-permute-start | bytes 12582920 | tf_op jit(solution)/shard_map/ppermute | solution.py:30
  169.9 48.2 %collective-permute-start.2 = (bf16[256,8192]{1,0:T(8,128)(2,1)}, bf16[256,8192]{1,0:T(8,128)(2,1)}, u32[]{:S(2)}, u32[]{:S(2)}) collective-permute-start(bf16[256,8192]{1,0:T(8,128)(2,1)} %collective-permute-done.1), channel_id=1, source_target_pairs={{0,2},{2,4},{4,6},{6,0},{1,3},{3,5},{5,7},{7,1},{8,10},{10,12},{12... | collective-permute-start | bytes 12582920 | tf_op jit(solution)/shard_map/ppermute | solution.py:30
  169.9 57.6 %copy-start.3 = (bf16[256,8192]{1,0:T(8,128)(2,1)S(1)}, bf16[256,8192]{1,0:T(8,128)(2,1)}, u32[]{:S(2)}) copy-start(bf16[256,8192]{1,0:T(8,128)(2,1)} %copy-done.2) | copy-start | bytes 12582916
  222.8 7.0 %copy-start.1 = (bf16[256,8192]{1,0:T(8,128)(2,1)S(1)}, bf16[256,8192]{1,0:T(8,128)(2,1)}, u32[]{:S(2)}) copy-start(bf16[256,8192]{1,0:T(8,128)(2,1)} %copy-done) | copy-start | bytes 12582916
Sparse Core Ops, SparseCore 0:
  28.3 26.2 all-reduce.5
  63.1 286.9 all-gather.1
  374.6 106.0 all-reduce.3
